TPU v7x, 128 devices: a whole 4x4x4 slice. The times are simulated.
128 devices in a mesh: row: 16 (over z, x), col: 8 (over y, core).
Axes of the slice: x: 4, y: 4, z: 4, core: 2. Of those that a mesh axis runs over, the one named last changes fastest.
Arguments:
- front: bfloat16 [128, 96, 256, 256], P('row', 'col'), may hold values from -1.5 to 1.5
- pattern: int32 [128, 96], replicated, may hold values from 0 to 1
- pivots: int32 [2], replicated, may hold values from 0 to 95, as said below
- pivot_inv: bfloat16 [2, 256, 256], replicated, may hold values from -0.09375 to 0.09375
Outputs:
- factored: bfloat16 [128, 96, 256, 256], P('row', 'col')
Inputs may be any that keep to these rules, and one draw needn't show every extreme that they name: The two pivots are distinct front block indices below 96; one of them is 95, the last block column of the window.
All inputs are finite; a program needn't handle non-finite values.
Results may differ from a plain program's by a relative error of at most 0.0051.
Values may be sent and summed in bfloat16 or wider, within the bound.
No kernel may reach another device: no remote copies, remote signals or barrier semaphores. Data moves between devices by JAX's collectives and lax.ppermute only.
A program may use at most 128 MiB of HBM per device.

v0:
```python
import jax
import jax.numpy as jnp
from jax import lax
from jax.sharding import PartitionSpec as P


def from_root(value, axis, source):
    kept = jnp.where(lax.axis_index(axis) == source, value, 0).astype(value.dtype)
    return lax.psum(kept, axis)


def lower_panel(matrix, pivot, inverse, rows_ok, ncol):
    column = lax.dynamic_index_in_dim(matrix, pivot // ncol, 1, keepdims=False)
    lower = jnp.einsum("iab,bc->iac", column, inverse, preferred_element_type=jnp.float32)
    lower = jnp.where(rows_ok[:, None, None], lower, 0.0).astype(jnp.bfloat16)
    return from_root(lower, "col", pivot % ncol)


def eliminate(matrix, lower, upper, pivot, rows_ok, cols_ok, local, front_cols):
    product = jnp.einsum("iab,jbc->ijac", lower, upper, preferred_element_type=jnp.float32)
    update = rows_ok[:, None] & cols_ok[None, :] & (local > 0)
    changed = (matrix.astype(jnp.float32) - product).astype(jnp.bfloat16)
    result = jnp.where(update[:, :, None, None], changed, matrix)
    place = rows_ok[:, None] & (front_cols == pivot)[None, :]
    return jnp.where(place[:, :, None, None], lower[:, None], result)


def body(front, pattern, pivots, pivot_inv):
    rows_dev = front.shape[0]
    cols_dev = front.shape[1]
    nrow = lax.axis_size("row")
    ncol = lax.axis_size("col")
    row_index = lax.axis_index("row")
    col_index = lax.axis_index("col")
    grid = pattern.reshape(rows_dev, nrow, cols_dev, ncol)
    local = lax.dynamic_index_in_dim(grid, row_index, 1, keepdims=False)
    local = lax.dynamic_index_in_dim(local, col_index, 2, keepdims=False)
    front_rows = jnp.arange(rows_dev, dtype=jnp.int32) * nrow + row_index
    front_cols = jnp.arange(cols_dev, dtype=jnp.int32) * ncol + col_index
    matrix = jnp.where(local[:, :, None, None] > 0, front, jnp.zeros_like(front))
    first = pivots[0]
    second = pivots[1]
    rows_first = front_rows != first
    cols_first = front_cols != first
    lower_first = lower_panel(matrix, first, pivot_inv[0], rows_first, ncol)
    first_row = lax.dynamic_index_in_dim(matrix, first // nrow, 0, keepdims=False)
    upper_first = from_root(first_row, "row", first % nrow)
    matrix = eliminate(
        matrix, lower_first, upper_first, first, rows_first, cols_first, local, front_cols
    )
    second_row = lax.dynamic_index_in_dim(matrix, second // nrow, 0, keepdims=False)
    upper_second = from_root(second_row, "row", second % nrow)
    rows_second = rows_first & (front_rows != second)
    cols_second = cols_first & (front_cols != second)
    lower_second = lower_panel(matrix, second, pivot_inv[1], rows_second, ncol)
    matrix = eliminate(
        matrix, lower_second, upper_second, second, rows_second, cols_second, local, front_cols
    )
    return matrix


def solution(mesh):
    placed = (P("row", "col", None, None), P(), P(), P())
    return jax.shard_map(
        body, mesh=mesh, in_specs=placed, out_specs=P("row", "col", None, None), check_vma=False
    )
```

profile of v0, /device:TPU:0, one launch (start us, length us, event | category | flops | bytes accessed | tf_op | source)
XLA Modules:
  0.0 411.9 jit_solution(12664829645244328995)
XLA Ops:
  6.5 0.0 all-reduce.5.cloned.1.call-start
  6.5 1.4 fusion.23
  10.3 0.6 fusion.22
  10.8 1.3 compare_and_fusion.1
  12.1 1.3 compare_and_fusion
  13.4 1.0 reshape.175
  14.4 0.1 constant_dynamic-slice_fusion
  14.5 0.1 copy.30
  14.6 16.6 %copy.22 = bf16[8,12,256,256]{2,3,1,0:T(8,128)(2,1)} copy(bf16[8,12,256,256]{3,2,1,0:T(8,128)(2,1)} %param.4) | data formatting | bytes 25165824 | tf_op args[0]
  31.2 0.1 and_and_fusion
  31.3 0.0 copy-start.1
  31.3 6.4 %broadcast_select_fusion = bf16[8,12,256,256]{2,3,1,0:T(8,128)(2,1)S(1)} fusion(bf16[8,12,256,256]{2,3,1,0:T(8,128)(2,1)} %copy.22, pred[8,12]{1,0:T(8,128)(4,1)S(1)} %get-tuple-element.6), kind=kLoop, calls=%fused_computation.8 | loop fusion | flops 6291456 | bytes 25165920 | tf_op jit(solution)/shard_map/jit(_where)/select_n | solution.py:40
  37.7 0.0 copy-start
  37.7 4.8 %copy-done = bf16[8,12,256,256]{2,3,1,0:T(8,128)(2,1)} copy-done((bf16[8,12,256,256]{2,3,1,0:T(8,128)(2,1)}, bf16[8,12,256,256]{2,3,1,0:T(8,128)(2,1)S(1)}, u32[]{:S(2)}) %copy-start) | copy-done | bytes 12582936
  42.5 0.0 copy-done.1
  42.5 1.6 fusion.8
  44.1 0.0 all-reduce.5.cloned.1.call-update
  44.1 0.0 all-reduce.7.cloned.1.call-start
  44.2 2.7 select_bitcast_fusion.1
  46.8 0.0 all-reduce.7.cloned.1.call-update
  46.9 0.0 all-reduce.9.cloned.1.call-start
  49.7 0.6 broadcast_compare_fusion
  50.3 0.1 broadcast_and_fusion
  50.4 58.8 %all-reduce.5.cloned.1.call-done = bf16[8,256,256]{2,1,0:T(8,128)(2,1)} async-done(((bf16[8,256,256]{2,1,0:T(8,128)(2,1)}), bf16[8,256,256]{2,1,0:T(8,128)(2,1)}) %all-reduce.5.cloned.1.call-update) | async-done | bytes 1048592 | tf_op jit(solution)/shard_map/psum | solution.py:9
  109.2 1.5 copy.24
  110.6 90.0 %all-reduce.7.cloned.1.call-done = bf16[12,256,256]{1,2,0:T(8,128)(2,1)} async-done(((bf16[12,256,256]{1,2,0:T(8,128)(2,1)}), bf16[12,256,256]{1,2,0:T(8,128)(2,1)}) %all-reduce.7.cloned.1.call-update) | async-done | bytes 1572880 | tf_op jit(solution)/shard_map/psum | solution.py:9
  200.6 16.1 %fusion.5 = bf16[8,12,256,256]{2,3,1,0:T(8,128)(2,1)} fusion(bf16[8,12,256,256]{2,3,1,0:T(8,128)(2,1)} %copy-done, pred[8,12]{1,0:T(8,128)(4,1)S(1)} %get-tuple-element.9, pred[8,12]{1,0:T(8,128)(4,1)S(1)} %get-tuple-element.8, bf16[8,256,256]{1,2,0:T(8,128)(2,1)S(1)} %copy.24, bf16[12,256,256]{1,2,0:T(8,128)(2,1)} %all-reduce.7.cloned.1.call-done, ...), kind=kOutput, calls=%fused_computation.7 | convolution fusion | flops 3252682752 | bytes 28836032 | tf_op jit(solution)/shard_map/iab,jbc->ijac/dot_general | solution.py:20
  216.7 2.8 fusion.9
  219.6 0.0 all-reduce.9.cloned.1.call-update
  219.6 0.0 all-reduce.11.cloned.1.call-start
  219.7 2.7 select_bitcast_fusion
  222.3 0.0 all-reduce.11.cloned.1.call-update
  222.4 59.1 %all-reduce.9.cloned.1.call-done = bf16[8,256,256]{2,1,0:T(8,128)(2,1)} async-done(((bf16[8,256,256]{2,1,0:T(8,128)(2,1)}), bf16[8,256,256]{2,1,0:T(8,128)(2,1)}) %all-reduce.9.cloned.1.call-update) | async-done | bytes 1048592 | tf_op jit(solution)/shard_map/psum | solution.py:9
  281.4 1.5 copy.26
  282.9 89.7 %all-reduce.11.cloned.1.call-done = bf16[12,256,256]{1,2,0:T(8,128)(2,1)} async-done(((bf16[12,256,256]{1,2,0:T(8,128)(2,1)}), bf16[12,256,256]{1,2,0:T(8,128)(2,1)}) %all-reduce.11.cloned.1.call-update) | async-done | bytes 1572880 | tf_op jit(solution)/shard_map/psum | solution.py:9
  372.6 16.1 %fusion.4 = bf16[8,12,256,256]{2,3,1,0:T(8,128)(2,1)} fusion(bf16[8,12,256,256]{2,3,1,0:T(8,128)(2,1)} %fusion.5, pred[8,12]{1,0:T(8,128)(4,1)S(1)} %get-tuple-element.5, pred[8,12]{1,0:T(8,128)(4,1)S(1)} %get-tuple-element.7, bf16[8,256,256]{1,2,0:T(8,128)(2,1)S(1)} %copy.26, bf16[12,256,256]{1,2,0:T(8,128)(2,1)} %all-reduce.11.cloned.1.call-done, ...), kind=kOutput, calls=%fused_computation.6 | convolution fusion | flops 3252682752 | bytes 28836032 | tf_op jit(solution)/shard_map/iab,jbc->ijac/dot_general | solution.py:20
  388.7 16.6 %copy.27 = bf16[8,12,256,256]{3,2,1,0:T(8,128)(2,1)} copy(bf16[8,12,256,256]{2,3,1,0:T(8,128)(2,1)} %fusion.4) | data formatting | bytes 25165824 | tf_op jit(solution)/shard_map/jit(_where)/select_n | solution.py:25
Async XLA Ops:
  6.5 102.6 %all-reduce.5.cloned.1.call-start = ((), (), s32[]{:S(2)}) async-start(), calls=%async_computation | async-start | bytes 2097152 | tf_op jit(solution)/shard_map/psum | solution.py:9
  31.3 11.2 %copy-start.1 = (bf16[2,256,256]{2,1,0:T(8,128)(2,1)S(1)}, bf16[2,256,256]{2,1,0:T(8,128)(2,1)}, u32[]{:S(2)}) copy-start(bf16[2,256,256]{2,1,0:T(8,128)(2,1)} %param.7) | copy-start | bytes 786436
  37.7 4.8 %copy-start = (bf16[8,12,256,256]{2,3,1,0:T(8,128)(2,1)}, bf16[8,12,256,256]{2,3,1,0:T(8,128)(2,1)S(1)}, u32[]{:S(2)}) copy-start(bf16[8,12,256,256]{2,3,1,0:T(8,128)(2,1)S(1)} %broadcast_select_fusion) | copy-start | bytes 37748740
  44.1 156.5 %all-reduce.7.cloned.1.call-start = ((), (), s32[]{:S(2)}) async-start(), calls=%async_computation.1 | async-start | bytes 3145728 | tf_op jit(solution)/shard_map/psum | solution.py:9
  46.9 234.6 %all-reduce.9.cloned.1.call-start = ((), (), s32[]{:S(2)}) async-start(), calls=%async_computation.2 | async-start | bytes 2097152 | tf_op jit(solution)/shard_map/psum | solution.py:9
  219.6 153.1 %all-reduce.11.cloned.1.call-start = ((), (), s32[]{:S(2)}) async-start(), calls=%async_computation.3 | async-start | bytes 3145728 | tf_op jit(solution)/shard_map/psum | solution.py:9
Sparse Core Ops, SparseCore 0:
  44.2 64.9 all-reduce.4
  112.5 88.0 all-reduce.6
  219.7 61.6 all-reduce.8
  284.6 88.0 all-reduce.10
where the time goes:
time: 413 us; the launch traced here: 412 us
  waiting for transfers between devices  298 us (72%)
  local copies, waits for them, and re-layouts  43.5 us (11%)
  matrix products  36.6 us (9%)
  between operations  18.4 us (4%)
  other arithmetic  15.6 us (4%)
    psum x4, waiting for transfers between devices, from_root(): return lax.psum(kept, axis)  298 us
    dot_general x2, matrix products, eliminate(): jnp.einsum('iab,jbc->ijac', lower, upper, preferred_element_type=jnp.floa...  32.2 us
    unnamed x6, local copies, waits for them, and re-layouts  21.5 us
    select_n x1, local copies, waits for them, and re-layouts, eliminate(): return jnp.where(place[:, :, None, None], lower[:, None], result)  16.6 us
  transfers between devices with their start and end apart: 4, of which 4 were waited for; matrix products, arithmetic and copies ran while one was open for 2% of the time, Pallas kernels for 0%

commit v1 on v0

--- a/solution.py
+++ b/solution.py
@@ -6,7 +6,7 @@
 
 def from_root(value, axis, source):
     kept = jnp.where(lax.axis_index(axis) == source, value, 0).astype(value.dtype)
-    return lax.psum(kept, axis)
+    return jnp.sum(lax.all_gather(kept, axis), axis=0)
 
 
 def lower_panel(matrix, pivot, inverse, rows_ok, ncol):

time: 413 us -> 542 us (1.31)
  waiting for transfers between devices: 298 us -> 393 us
  other arithmetic: 15.6 us -> 56 us
    all_gather x0 -> x4, waiting for transfers between devices: none -> 393 us  [from_root(): return jnp.sum(lax.all_gather(kept, axis), axis=0)]
    psum x4 -> x0, waiting for transfers between devices: 298 us -> none  [from_root(): return lax.psum(kept, axis)]
    reduce_sum x0 -> x4, other arithmetic: none -> 36.1 us  [from_root(): return jnp.sum(lax.all_gather(kept, axis), axis=0)]
    unnamed x6 -> x4, local copies, waits for them, and re-layouts: 21.5 us -> 16.8 us
  transfers between devices with their start and end apart: 4 -> 4, of which waited for: 4 -> 4; matrix products, arithmetic and copies ran while one was open for 2% -> 4% of each run, Pallas kernels for 0% -> 0%
where the time goes in v1:
time: 542 us; the launch traced here: 540 us
  waiting for transfers between devices  393 us (73%)
  other arithmetic  56 us (10%)
  local copies, waits for them, and re-layouts  38.9 us (7%)
  matrix products  33.4 us (6%)
  between operations  18.2 us (3%)
    all_gather x4, waiting for transfers between devices, from_root(): return jnp.sum(lax.all_gather(kept, axis), axis=0)  393 us
    reduce_sum x4, other arithmetic, from_root(): return jnp.sum(lax.all_gather(kept, axis), axis=0)  36.1 us
    dot_general x2, matrix products, eliminate(): jnp.einsum('iab,jbc->ijac', lower, upper, preferred_element_type=jnp.floa...  27.8 us
    unnamed x4, local copies, waits for them, and re-layouts  16.8 us
    select_n x1, local copies, waits for them, and re-layouts, eliminate(): return jnp.where(place[:, :, None, None], lower[:, None], result)  16.6 us
  transfers between devices with their start and end apart: 4, of which 4 were waited for; matrix products, arithmetic and copies ran while one was open for 4% of the time, Pallas kernels for 0%

profile of v1, /device:TPU:0, one launch (start us, length us, event | category | flops | bytes accessed | tf_op | source)
XLA Modules:
  0.0 539.8 jit_solution(3914503028723430341)
XLA Ops:
  6.5 0.0 all-gather.11.cloned.1.call-start
  6.5 1.3 fusion.23
  9.7 1.2 compare_and_fusion
  10.9 1.2 compare_and_fusion.1
  12.8 0.6 fusion.22
  13.4 1.0 reshape.169
  14.4 0.1 constant_dynamic-slice_fusion
  14.5 0.1 copy.53
  14.6 0.1 and_and_fusion
  14.7 0.1 copy.42
  14.8 16.6 %copy.43 = bf16[8,12,256,256]{2,3,0,1:T(8,128)(2,1)} copy(bf16[8,12,256,256]{3,2,1,0:T(8,128)(2,1)} %param.4) | data formatting | bytes 25165824 | tf_op args[0]
  31.4 0.0 copy-start
  31.4 10.7 %broadcast_select_fusion = bf16[8,12,256,256]{2,3,0,1:T(8,128)(2,1)} fusion(bf16[8,12,256,256]{2,3,0,1:T(8,128)(2,1)} %copy.43, pred[8,12]{0,1:T(8,128)(4,1)S(1)} %copy.42), kind=kLoop, calls=%fused_computation.8 | loop fusion | flops 6291456 | bytes 25165920 | tf_op jit(solution)/shard_map/jit(_where)/select_n | solution.py:40
  42.1 0.0 copy-done
  42.1 2.8 fusion.8
  44.9 0.0 all-gather.11.cloned.1.call-update
  44.9 0.0 all-gather.7.cloned.1.call-start
  45.0 2.7 dynamic-slice_select_fusion.1
  47.7 0.0 all-gather.7.cloned.1.call-update
  47.7 0.0 all-gather.13.cloned.1.call-start
  50.2 0.6 broadcast_compare_fusion
  50.9 0.1 broadcast_and_fusion
  50.9 0.1 copy.40
  51.0 0.1 copy.46
  51.1 46.1 %all-gather.11.cloned.1.call-done = bf16[64,256,256]{2,1,0:T(8,128)(2,1)} async-done(((bf16[8,256,256]{2,1,0:T(8,128)(2,1)}), bf16[64,256,256]{2,1,0:T(8,128)(2,1)}) %all-gather.11.cloned.1.call-update) | async-done | bytes 8388624 | tf_op jit(solution)/shard_map/all_gather | solution.py:9
  97.3 5.0 reduce_sum.48
  102.3 1.4 copy.45
  103.6 150.3 %all-gather.7.cloned.1.call-done = bf16[16,12,256,256]{2,3,0,1:T(8,128)(2,1)} async-done(((bf16[1,12,256,256]{2,3,0,1:T(8,128)(2,1)}), bf16[16,12,256,256]{2,3,0,1:T(8,128)(2,1)}) %all-gather.7.cloned.1.call-update) | async-done | bytes 25165840 | tf_op jit(solution)/shard_map/all_gather | solution.py:9
  253.9 13.0 %reduce_sum.49 = bf16[12,256,256]{1,2,0:T(8,128)(2,1)S(1)} reduce(bf16[16,12,256,256]{2,3,0,1:T(8,128)(2,1)} %all-gather.7.cloned.1.call-done, bf16[]{:T(256)} %constant.124.clone.1), dimensions={0}, to_apply=%region_1.2 | reduce | flops 11796480 | bytes 26738690 | tf_op jit(solution)/shard_map/reduce_sum | solution.py:9
  267.0 13.9 %fusion.5 = bf16[8,12,256,256]{2,3,0,1:T(8,128)(2,1)} fusion(bf16[8,12,256,256]{2,3,0,1:T(8,128)(2,1)} %broadcast_select_fusion, pred[8,12]{0,1:T(8,128)(4,1)S(1)} %copy.46, pred[8,12]{0,1:T(8,128)(4,1)S(1)} %copy.40, bf16[8,256,256]{1,2,0:T(8,128)(2,1)} %copy.45, bf16[12,256,256]{1,2,0:T(8,128)(2,1)S(1)} %reduce_sum.49, bf16[8,256,256]{2,1,0:T(8,128)(2,1)S(1)} %reduce_sum.48), kind=kOutput, calls=%fused_computation.7 | convolution fusion | flops 3252682752 | bytes 28836032 | tf_op jit(solution)/shard_map/iab,jbc->ijac/dot_general | solution.py:20
  280.9 2.8 fusion.9
  283.7 0.0 all-gather.13.cloned.1.call-update
  283.7 0.2 all-gather.9.cloned.1.call-start
  284.0 2.7 dynamic-slice_select_fusion
  286.7 0.0 all-gather.9.cloned.1.call-update
  286.7 0.1 copy.39
  286.8 0.1 copy.49
  286.9 46.3 %all-gather.13.cloned.1.call-done = bf16[64,256,256]{2,1,0:T(8,128)(2,1)} async-done(((bf16[8,256,256]{2,1,0:T(8,128)(2,1)}), bf16[64,256,256]{2,1,0:T(8,128)(2,1)}) %all-gather.13.cloned.1.call-update) | async-done | bytes 8388624 | tf_op jit(solution)/shard_map/all_gather | solution.py:9
  333.2 5.0 reduce_sum.50
  338.3 1.4 copy.48
  339.6 150.1 %all-gather.9.cloned.1.call-done = bf16[16,12,256,256]{2,3,0,1:T(8,128)(2,1)} async-done(((bf16[1,12,256,256]{2,3,0,1:T(8,128)(2,1)}), bf16[16,12,256,256]{2,3,0,1:T(8,128)(2,1)}) %all-gather.9.cloned.1.call-update) | async-done | bytes 25165840 | tf_op jit(solution)/shard_map/all_gather | solution.py:9
  489.8 13.0 %reduce_sum.51 = bf16[12,256,256]{1,2,0:T(8,128)(2,1)S(1)} reduce(bf16[16,12,256,256]{2,3,0,1:T(8,128)(2,1)} %all-gather.9.cloned.1.call-done, bf16[]{:T(256)} %constant.124.clone.1), dimensions={0}, to_apply=%region_3.4 | reduce | flops 11796480 | bytes 26738690 | tf_op jit(solution)/shard_map/reduce_sum | solution.py:9
  502.8 13.8 %fusion.4 = bf16[8,12,256,256]{2,3,0,1:T(8,128)(2,1)} fusion(bf16[8,12,256,256]{2,3,0,1:T(8,128)(2,1)} %fusion.5, pred[8,12]{0,1:T(8,128)(4,1)S(1)} %copy.49, pred[8,12]{0,1:T(8,128)(4,1)S(1)} %copy.39, bf16[8,256,256]{1,2,0:T(8,128)(2,1)} %copy.48, bf16[12,256,256]{1,2,0:T(8,128)(2,1)S(1)} %reduce_sum.51, bf16[8,256,256]{2,1,0:T(8,128)(2,1)S(1)} %reduce_sum.50), kind=kOutput, calls=%fused_computation.6 | convolution fusion | flops 3252682752 | bytes 28836032 | tf_op jit(solution)/shard_map/iab,jbc->ijac/dot_general | solution.py:20
  516.7 16.6 %copy.50 = bf16[8,12,256,256]{3,2,1,0:T(8,128)(2,1)} copy(bf16[8,12,256,256]{2,3,0,1:T(8,128)(2,1)} %fusion.4) | data formatting | bytes 25165824 | tf_op jit(solution)/shard_map/jit(_where)/select_n | solution.py:25
Async XLA Ops:
  6.5 90.7 %all-gather.11.cloned.1.call-start = ((), (), s32[]{:S(2)}) async-start(), calls=%async_computation.2 | async-start | bytes 9437184 | tf_op jit(solution)/shard_map/all_gather | solution.py:9
  31.4 10.7 %copy-start = (bf16[2,256,256]{2,1,0:T(8,128)(2,1)S(1)}, bf16[2,256,256]{2,1,0:T(8,128)(2,1)}, u32[]{:S(2)}) copy-start(bf16[2,256,256]{2,1,0:T(8,128)(2,1)} %param.7) | copy-start | bytes 786436
  44.9 209.0 %all-gather.7.cloned.1.call-start = ((), (), s32[]{:S(2)}) async-start(), calls=%async_computation | async-start | bytes 26738688 | tf_op jit(solution)/shard_map/all_gather | solution.py:9
  47.7 285.6 %all-gather.13.cloned.1.call-start = ((), (), s32[]{:S(2)}) async-start(), calls=%async_computation.3 | async-start | bytes 9437184 | tf_op jit(solution)/shard_map/all_gather | solution.py:9
  283.7 206.0 %all-gather.9.cloned.1.call-start = ((), (), s32[]{:S(2)}) async-start(), calls=%async_computation.1 | async-start | bytes 26738688 | tf_op jit(solution)/shard_map/all_gather | solution.py:9
Sparse Core Ops, SparseCore 0:
  45.0 52.1 all-gather.10
  99.4 154.4 all-gather.6
  283.9 49.3 all-gather.12
  335.2 154.4 all-gather.8
